TPU v7x, 512 devices: a whole 4x8x8 slice. The times are simulated.
512 devices in a mesh: prompt: 32 (over x, y), sample: 16 (over z, core).
Axes of the slice: x: 4, y: 8, z: 8, core: 2. Of those that a mesh axis runs over, the one named last changes fastest.
Arguments:
- queries: bfloat16 [32, 16, 4, 8192], P('prompt', 'sample'), may hold values from -24 to 24
- new_kv: bfloat16 [32, 16, 4, 2, 1024], P('prompt', 'sample'), may hold values from -24 to 24
- suffix_kv: bfloat16 [32, 16, 256, 2, 1024], P('prompt', 'sample'), may hold values from -24 to 24
- suffix_len: int32 [32, 16], P('prompt', 'sample'), may hold values from 1 to 256, as said below
- prefix_head: bfloat16 [32, 2048, 2, 1024], P('prompt', 'sample'), may hold values from -24 to 24
- prefix_tail: bfloat16 [32, 2048, 2, 1024], P('prompt', 'sample'), may hold values from -24 to 24
- prefix_len: int32 [32], replicated, may hold values from 1024 to 4096, as said below
Outputs:
- attended: bfloat16 [32, 16, 4, 8192], P('prompt', 'sample')
Inputs may be any that keep to these rules, and one draw needn't show every extreme that they name: `suffix_len`: some sample has all 256 slots live and some only one. `prefix_len`: some prompt has all 4096 positions live and some only 1024.
All inputs are finite; a program needn't handle non-finite values.
Results may differ from a plain program's by a relative error of at most 0.001.
Values may be sent and summed in bfloat16 or wider, within the bound.
No kernel may reach another device: no remote copies, remote signals or barrier semaphores. Data moves between devices by JAX's collectives and lax.ppermute only.
A program may use at most 64 MiB of HBM per device.

v0:
```python
import jax
import jax.numpy as jnp
from jax import lax
from jax.sharding import PartitionSpec as P

QH = 64
KVH = 8
HEAD_SIZE = 128
NEG = -1e30


def from_behind(value, axis, steps):
    count = lax.axis_size(axis)
    pairs = [(source, (source + steps) % count) for source in range(count)]
    return lax.ppermute(value, axis, pairs)


def apply_weights(logit_scores, valid_mask, value_matrix, form):
    masked = jnp.where(valid_mask, logit_scores, NEG)
    maxima = jnp.max(masked, axis=-1)
    weights = jnp.where(valid_mask, jnp.exp(masked - maxima[..., None]), 0.0)
    totals = jnp.sum(weights, axis=-1)
    numerator = jnp.einsum(form, weights, value_matrix, precision=lax.Precision.HIGHEST)
    leading = numerator.shape[:2]
    return (
        numerator.reshape(leading + (QH, HEAD_SIZE)),
        maxima.reshape(leading + (QH,)),
        totals.reshape(leading + (QH,)),
    )


def prefix_terms(query_rows, pairs, start, length):
    sample_count, step_count = (query_rows.shape[0], query_rows.shape[1])
    block_len = pairs.shape[0]
    grouped_queries = query_rows.reshape(sample_count, step_count, KVH, QH // KVH, HEAD_SIZE)
    key_matrix = pairs[:, 0].reshape(block_len, KVH, HEAD_SIZE)
    value_matrix = pairs[:, 1].reshape(block_len, KVH, HEAD_SIZE).astype(jnp.float32)
    logit_scores = jnp.einsum(
        "rhlxf,vlf->rhlxv", grouped_queries, key_matrix, preferred_element_type=jnp.float32
    ) * HEAD_SIZE ** (-0.5)
    valid_mask = start + jnp.arange(block_len, dtype=jnp.int32) < length
    return apply_weights(logit_scores, valid_mask, value_matrix, "urpyj,jpi->urpyi")


def suffix_terms(query_rows, cache, fresh, length):
    sample_count, step_count = (query_rows.shape[0], query_rows.shape[1])
    slots = cache.shape[1]
    joined = jnp.concatenate([cache, fresh], axis=1)
    total_len = joined.shape[1]
    grouped_queries = query_rows.reshape(sample_count, step_count, KVH, QH // KVH, HEAD_SIZE)
    key_matrix = joined[:, :, 0].reshape(sample_count, total_len, KVH, HEAD_SIZE)
    value_matrix = (
        joined[:, :, 1].reshape(sample_count, total_len, KVH, HEAD_SIZE).astype(jnp.float32)
    )
    logit_scores = jnp.einsum(
        "stkgd,slkd->stkgl", grouped_queries, key_matrix, preferred_element_type=jnp.float32
    ) * HEAD_SIZE ** (-0.5)
    cache_live = jnp.arange(slots, dtype=jnp.int32)[None, :] < length[:, None]
    steps_live = (
        jnp.arange(step_count, dtype=jnp.int32)[None, :]
        <= jnp.arange(step_count, dtype=jnp.int32)[:, None]
    )
    valid_mask = jnp.concatenate(
        [
            jnp.broadcast_to(cache_live[:, None, :], (sample_count, step_count, slots)),
            steps_live[None],
        ],
        axis=2,
    )
    return apply_weights(
        logit_scores, valid_mask[:, :, None, None, :], value_matrix, "stkgl,slkd->stkgd"
    )


def join(former, latter):
    maxima = jnp.maximum(former[1], latter[1])
    scale_a = jnp.exp(former[1] - maxima)
    scale_b = jnp.exp(latter[1] - maxima)
    return (
        former[0] * scale_a[..., None] + latter[0] * scale_b[..., None],
        maxima,
        former[2] * scale_a + latter[2] * scale_b,
    )


def settle(stacked):
    maxima = jnp.max(stacked[1], axis=0)
    factors = jnp.exp(stacked[1] - maxima[None])
    return (
        jnp.sum(stacked[0] * factors[..., None], axis=0),
        maxima,
        jnp.sum(stacked[2] * factors, axis=0),
    )


def spread(partial_sums):
    return (
        lax.all_to_all(partial_sums[0][None], "sample", split_axis=1, concat_axis=0, tiled=True),
        lax.all_to_all(partial_sums[1][None], "sample", split_axis=1, concat_axis=0, tiled=True),
        lax.all_to_all(partial_sums[2][None], "sample", split_axis=1, concat_axis=0, tiled=True),
    )


def per_device(queries, new_kv, suffix_kv, suffix_len, prefix_head, prefix_tail, prefix_len):
    sample_count = lax.axis_size("sample")
    prompt_row = lax.axis_index("prompt")
    sample_slot = lax.axis_index("sample")
    block_len = prefix_head.shape[1]
    half_len = block_len * sample_count
    own_length = prefix_len[prompt_row]
    local_rows = queries[0]
    every_rows = lax.all_gather(queries, "sample", axis=1, tiled=True)[0]
    near_part = suffix_terms(local_rows, suffix_kv[0], new_kv[0], suffix_len[0])
    moved = from_behind(prefix_tail, "prompt", -1)
    own_part = prefix_terms(every_rows, prefix_head[0], sample_slot * block_len, own_length)
    tail_part = prefix_terms(every_rows, moved[0], half_len + sample_slot * block_len, own_length)
    result = join(settle(spread(join(own_part, tail_part))), near_part)
    attended = (result[0] / result[2][..., None]).astype(jnp.bfloat16)
    return attended.reshape(queries.shape)


def solution(mesh):
    in_specs = (
        P("prompt", "sample", None, None),
        P("prompt", "sample", None, None, None),
        P("prompt", "sample", None, None, None),
        P("prompt", "sample"),
        P("prompt", "sample", None, None),
        P("prompt", "sample", None, None),
        P(),
    )
    out_specs = P("prompt", "sample", None, None)
    return jax.shard_map(
        per_device, mesh=mesh, in_specs=in_specs, out_specs=out_specs, check_vma=False
    )
```

profile of v0, /device:TPU:1, one launch (start us, length us, event | category | flops | bytes accessed | tf_op | source)
XLA Modules:
  0.0 154.0 jit_solution(10899200841303403284)
XLA Ops:
  6.5 0.7 all-gather.2.cloned.1.call-update
  7.3 1.4 copy.107
  8.6 8.1 %collective-permute-start = (bf16[1,128,2,1024]{1,3,2,0:T(8,128)(2,1)S(1)}, bf16[1,128,2,1024]{1,3,2,0:T(8,128)(2,1)S(1)}, u32[]{:S(2)}, u32[]{:S(2)}) collective-permute-start(bf16[1,128,2,1024]{1,3,2,0:T(8,128)(2,1)S(1)} %copy.107), channel_id=1, source_target_pairs={{0,496},{16,0},{32,16},{48,32},{64,48},{80,64},{96,80},{112,96},{1... | collective-permute-start | bytes 1572872 | tf_op jit(solution)/shard_map/ppermute | solution.py:15
  16.8 1.4 copy.98
  20.1 7.2 %collective-permute-done = bf16[1,128,2,1024]{1,3,2,0:T(8,128)(2,1)S(1)} collective-permute-done((bf16[1,128,2,1024]{1,3,2,0:T(8,128)(2,1)S(1)}, bf16[1,128,2,1024]{1,3,2,0:T(8,128)(2,1)S(1)}, u32[]{:S(2)}, u32[]{:S(2)}) %collective-permute-start) | collective-permute-done | bytes 524320 | tf_op jit(solution)/shard_map/ppermute | solution.py:15
  27.4 30.0 %all-gather.2.cloned.1.call-done = bf16[1,16,4,8192]{3,2,0,1:T(4,128)(2,1)} async-done(((bf16[1,1,4,8192]{3,2,0,1:T(4,128)(2,1)}), bf16[1,16,4,8192]{3,2,0,1:T(4,128)(2,1)}) %all-gather.2.cloned.1.call-update) | async-done | bytes 1048592 | tf_op jit(solution)/shard_map/all_gather | solution.py:112
  57.4 2.1 %reshape.433 = bf16[16,4,8,8,128]{4,3,2,1,0:T(8,128)(2,1)S(1)} reshape(bf16[1,16,4,8192]{3,2,0,1:T(4,128)(2,1)} %all-gather.2.cloned.1.call-done) | data formatting | bytes 2097152 | tf_op jit(solution)/shard_map/reshape;squeeze | solution.py:35
  59.5 1.0 bitcast_reduce_fusion
  60.6 1.0 bitcast_reduce_fusion.1
  61.6 3.3 %fusion.47 = (f32[16,4,8,8]{0,3,1,2:T(8,128)S(1)}, f32[16,4,8,8,128]{4,0,3,1,2:T(8,128)}, f32[16,4,8,8]{0,3,1,2:T(8,128)S(1)}, f32[16,4,8,8,128]{4,0,3,1,2:T(8,128)}) fusion(f32[16,4,8,8]{0,3,1,2:T(8,128)S(1)} %get-tuple-element.26, f32[8,128,16,4,8]{1,2,4,3,0:T(8,128)S(1)} %get-tuple-element.27, pred[128]{0:T(512)(128)(4,1)S(1)} %add_compare_fusion.1, ...), kind=kLoop, calls=%fused_computation.79 | loop fusion | flops 5234688 | bytes 8454400 | tf_op jit(solution)/shard_map/reduce_sum | solution.py:22
  65.0 0.7 reshape.437
  65.7 4.5 %all-to-all-start.1 = ((f32[16,1,256]{2,1,0:T(1,128)}), f32[16,1,256]{2,1,0:T(1,128)S(1)}, u32[]{:S(2)}, u32[]{:S(2)}) async-start(f32[16,1,256]{2,1,0:T(1,128)} %reshape.437), calls=%async_computation.1 | async-start | bytes 32768 | tf_op jit(solution)/shard_map/all_to_all | solution.py:99
  70.4 3.4 %fusion.11 = f32[16,4,8,8,128]{4,3,1,0,2:T(8,128)S(1)} fusion(bf16[128,8,128,1,1]{0,2,4,3,1:T(8,128)(2,1)S(1)} %bitcast.166, f32[16,4,8,8,128]{4,0,3,1,2:T(8,128)} %get-tuple-element.11), kind=kOutput, calls=%fused_computation.20 | convolution fusion | flops 805306368 | bytes 4456448 | tf_op jit(solution)/shard_map/urpyj,jpi->urpyi/dot_general | solution.py:23
  73.8 3.1 %fusion.14 = f32[16,4,8,8,128]{4,3,1,0,2:T(8,128)} fusion(bf16[128,8,128,1,1]{0,2,4,3,1:T(8,128)(2,1)S(1)} %bitcast.167, f32[16,4,8,8,128]{4,0,3,1,2:T(8,128)S(1)} %copy-done), kind=kOutput, calls=%fused_computation.21 | convolution fusion | flops 805306368 | bytes 4456448 | tf_op jit(solution)/shard_map/urpyj,jpi->urpyi/dot_general | solution.py:23
  77.0 0.7 reshape.439
  77.7 7.2 %all-to-all-start.2 = ((f32[16,1,256]{2,1,0:T(1,128)}), f32[16,1,256]{2,1,0:T(1,128)S(1)}, u32[]{:S(2)}, u32[]{:S(2)}) async-start(f32[16,1,256]{2,1,0:T(1,128)} %reshape.439), calls=%async_computation.2 | async-start | bytes 32768 | tf_op jit(solution)/shard_map/all_to_all | solution.py:100
  84.9 3.4 %fusion.2 = f32[1,16,4,64,128]{4,3,2,0,1:T(8,128)} fusion(f32[16,4,8,8,128]{4,3,1,0,2:T(8,128)} %fusion.14, f32[16,4,8,8,128]{4,3,1,0,2:T(8,128)S(1)} %fusion.11, f32[16,4,64]{2,1,0:T(4,128)S(1)} %copy.119, f32[16,4,64]{2,1,0:T(4,128)S(1)} %copy.114), kind=kLoop, calls=%fused_computation.4 | loop fusion | flops 1572864 | bytes 6324224 | tf_op jit(solution)/shard_map/add | solution.py:80
  88.4 3.9 %all-to-all-done.2 = f32[16,1,256]{2,1,0:T(1,128)S(1)} async-done(((f32[16,1,256]{2,1,0:T(1,128)}), f32[16,1,256]{2,1,0:T(1,128)S(1)}, u32[]{:S(2)}, u32[]{:S(2)}) %all-to-all-start.2) | async-done | bytes 16416 | tf_op jit(solution)/shard_map/all_to_all | solution.py:100
  92.3 3.9 %all-to-all-start = ((f32[1,16,4,64,128]{4,3,2,0,1:T(8,128)}), f32[1,16,4,64,128]{4,3,2,0,1:T(8,128)S(1)}, u32[]{:S(2)}, u32[]{:S(2)}) async-start(f32[1,16,4,64,128]{4,3,2,0,1:T(8,128)} %fusion.2), calls=%async_computation | async-start | bytes 4194304 | tf_op jit(solution)/shard_map/all_to_all | solution.py:98
  96.8 12.8 %fusion.19 = (bf16[260,1024]{1,0:T(8,128)(2,1)S(1)}, bf16[260,1024]{1,0:T(8,128)(2,1)S(1)}) fusion(bf16[1,4,2,1024]{3,2,1,0:T(2,128)(2,1)S(1)} %bitcast.181, bf16[1,256,2,1024]{3,2,1,0:T(2,128)(2,1)} %bitcast.165), kind=kLoop, calls=%fused_computation.28 | loop fusion | flops 2129920 | bytes 2129920 | tf_op jit(solution)/shard_map/slice | solution.py:53
  112.6 0.7 reduce.11
  113.5 31.7 %all-to-all-done = f32[1,16,4,64,128]{4,3,2,0,1:T(8,128)S(1)} async-done(((f32[1,16,4,64,128]{4,3,2,0,1:T(8,128)}), f32[1,16,4,64,128]{4,3,2,0,1:T(8,128)S(1)}, u32[]{:S(2)}, u32[]{:S(2)}) %all-to-all-start) | async-done | bytes 2097184 | tf_op jit(solution)/shard_map/all_to_all | solution.py:98
  145.2 0.7 fusion
  146.4 0.7 copy.133
  (53 shorter events, 6.1 us)
Async XLA Ops:
  6.5 11.6 %copy-start.3 = (s32[32]{0:T(128)S(1)}, s32[32]{0:T(128)}, u32[]{:S(2)}) copy-start(s32[32]{0:T(128)} %param.13) | copy-start | bytes 388
  6.5 50.8 %all-gather.2.cloned.1.call-start = ((), (), s32[]{:S(2)}) async-start(), calls=%async_computation.3 | async-start | bytes 1114112 | tf_op jit(solution)/shard_map/all_gather | solution.py:112
  8.6 18.7 %collective-permute-start = (bf16[1,128,2,1024]{1,3,2,0:T(8,128)(2,1)S(1)}, bf16[1,128,2,1024]{1,3,2,0:T(8,128)(2,1)S(1)}, u32[]{:S(2)}, u32[]{:S(2)}) collective-permute-start(bf16[1,128,2,1024]{1,3,2,0:T(8,128)(2,1)S(1)} %copy.107), channel_id=1, source_target_pairs={{0,496},{16,0},{32,16},{48,32},{64,48},{80,64},{96,80},{112,96},{1... | collective-permute-start | bytes 1572872 | tf_op jit(solution)/shard_map/ppermute | solution.py:15
  65.7 12.0 %all-to-all-start.1 = ((f32[16,1,256]{2,1,0:T(1,128)}), f32[16,1,256]{2,1,0:T(1,128)S(1)}, u32[]{:S(2)}, u32[]{:S(2)}) async-start(f32[16,1,256]{2,1,0:T(1,128)} %reshape.437), calls=%async_computation.1 | async-start | bytes 32768 | tf_op jit(solution)/shard_map/all_to_all | solution.py:99
  70.4 3.4 %copy-start = (f32[16,4,8,8,128]{4,0,3,1,2:T(8,128)S(1)}, f32[16,4,8,8,128]{4,0,3,1,2:T(8,128)}, u32[]{:S(2)}) copy-start(f32[16,4,8,8,128]{4,0,3,1,2:T(8,128)} %get-tuple-element.29) | copy-start | bytes 6291460
  77.7 14.6 %all-to-all-start.2 = ((f32[16,1,256]{2,1,0:T(1,128)}), f32[16,1,256]{2,1,0:T(1,128)S(1)}, u32[]{:S(2)}, u32[]{:S(2)}) async-start(f32[16,1,256]{2,1,0:T(1,128)} %reshape.439), calls=%async_computation.2 | async-start | bytes 32768 | tf_op jit(solution)/shard_map/all_to_all | solution.py:100
  88.4 8.4 %copy-start.2 = (bf16[1,1,4,2,1024]{4,3,2,1,0:T(2,128)(2,1)S(1)}, bf16[1,1,4,2,1024]{4,3,2,1,0:T(2,128)(2,1)}, u32[]{:S(2)}) copy-start(bf16[1,1,4,2,1024]{4,3,2,1,0:T(2,128)(2,1)} %param.8) | copy-start | bytes 49156
  92.3 52.9 %all-to-all-start = ((f32[1,16,4,64,128]{4,3,2,0,1:T(8,128)}), f32[1,16,4,64,128]{4,3,2,0,1:T(8,128)S(1)}, u32[]{:S(2)}, u32[]{:S(2)}) async-start(f32[1,16,4,64,128]{4,3,2,0,1:T(8,128)} %fusion.2), calls=%async_computation | async-start | bytes 4194304 | tf_op jit(solution)/shard_map/all_to_all | solution.py:98
  96.8 13.0 %copy-start.1 = (bf16[1,1,4,8192]{3,2,1,0:T(4,128)(2,1)S(1)}, bf16[1,1,4,8192]{3,2,1,0:T(4,128)(2,1)}, u32[]{:S(2)}) copy-start(bf16[1,1,4,8192]{3,2,1,0:T(4,128)(2,1)} %param.7) | copy-start | bytes 196612
Sparse Core Ops, SparseCore 0:
  9.5 47.8 all-gather.1
where the time goes:
time: 154 us
  waiting for transfers between devices  73.5 us (48%)
  starting transfers between devices  23.7 us (15%)
  other arithmetic  23.6 us (15%)
  between operations  14.4 us (9%)
  matrix products  9.42 us (6%)
  local copies, waits for them, and re-layouts  9.41 us (6%)
    all_to_all x1, waiting for transfers between devices, spread(): lax.all_to_all(partial_sums[0][None], 'sample', split_axis=1, concat_axis...  31.7 us
    all_gather x1, waiting for transfers between devices, per_device(): every_rows = lax.all_gather(queries, 'sample', axis=1, tiled=True)[0]  30 us
    slice x1, other arithmetic, suffix_terms(): joined[:, :, 1].reshape(sample_count, total_len, KVH, HEAD_SIZE)  12.8 us
    ppermute x1, starting transfers between devices, from_behind(): return lax.ppermute(value, axis, pairs)  8.12 us
    all_to_all x1, starting transfers between devices, spread(): lax.all_to_all(partial_sums[2][None], 'sample', split_axis=1, concat_axis...  7.22 us
    ppermute x1, waiting for transfers between devices, from_behind(): return lax.ppermute(value, axis, pairs)  7.22 us
    dot_general x3, matrix products, apply_weights(): jnp.einsum(form, weights, value_matrix, precision=lax.Precision.HIGHEST)  7.01 us
    unnamed x16, local copies, waits for them, and re-layouts  4.55 us
  transfers between devices with their start and end apart: 5, of which 4 were waited for; matrix products, arithmetic and copies ran while one was open for 21% of the time, Pallas kernels for 0%

commit v1 on v0

--- a/solution.py
+++ b/solution.py
@@ -7,6 +7,17 @@
 KVH = 8
 HEAD_SIZE = 128
 NEG = -1e30
+
+
+def _place_lines(message):
+    w_next = lax.all_to_all(
+        jnp.stack([message] * lax.axis_size("sample"), axis=0),
+        axis_name="sample",
+        split_axis=0,
+        concat_axis=0,
+    )
+    found_now = jnp.concatenate(w_next, axis=1)
+    return found_now
 
 
 def from_behind(value, axis, steps):
@@ -109,7 +120,7 @@
     half_len = block_len * sample_count
     own_length = prefix_len[prompt_row]
     local_rows = queries[0]
-    every_rows = lax.all_gather(queries, "sample", axis=1, tiled=True)[0]
+    every_rows = _place_lines(queries)[0]
     near_part = suffix_terms(local_rows, suffix_kv[0], new_kv[0], suffix_len[0])
     moved = from_behind(prefix_tail, "prompt", -1)
     own_part = prefix_terms(every_rows, prefix_head[0], sample_slot * block_len, own_length)

time: 154 us -> 131 us (0.85)
  waiting for transfers between devices: 73.5 us -> 51.8 us
  between operations: 14.4 us -> 0.98 us
  starting transfers between devices: 23.7 us -> 33.9 us
    all_gather x1 -> x0, waiting for transfers between devices: 30 us -> none  [per_device(): every_rows = lax.all_gather(queries, 'sample', axis=1, tiled=True)[0]]
    all_to_all x0 -> x1, starting transfers between devices: none -> 12 us  [_place_lines(): lax.all_to_all(jnp.stack([message] * lax.axis_size('sample'), axis=0), ax...]
    all_to_all x0 -> x1, waiting for transfers between devices: none -> 7.12 us  [_place_lines(): lax.all_to_all(jnp.stack([message] * lax.axis_size('sample'), axis=0), ax...]
    another operation x2 -> x3, local copies, waits for them, and re-layouts: 0.07 us -> 2.4 us  [the longest x1 2.32 us: _place_lines(): jnp.stack([message] * lax.axis_size('sample'), axis=0)]
    ppermute x1, waiting for transfers between devices: 7.22 us -> 9.04 us  [from_behind(): return lax.ppermute(value, axis, pairs)]
    unnamed x16 -> x22, local copies, waits for them, and re-layouts: 4.55 us -> 3.53 us
  transfers between devices with their start and end apart: 5 -> 5, of which waited for: 4 -> 4; matrix products, arithmetic and copies ran while one was open for 21% -> 24% of each run, Pallas kernels for 0% -> 0%
where the time goes in v1:
time: 131 us; the launch traced here: 130 us
  waiting for transfers between devices  51.8 us (40%)
  starting transfers between devices  33.9 us (26%)
  other arithmetic  23.6 us (18%)
  local copies, waits for them, and re-layouts  10.4 us (8%)
  matrix products  9.42 us (7%)
    all_to_all x1, waiting for transfers between devices, spread(): lax.all_to_all(partial_sums[0][None], 'sample', split_axis=1, concat_axis...  31.7 us
    slice x1, other arithmetic, suffix_terms(): joined[:, :, 1].reshape(sample_count, total_len, KVH, HEAD_SIZE)  12.7 us
    all_to_all x1, starting transfers between devices, _place_lines(): lax.all_to_all(jnp.stack([message] * lax.axis_size('sample'), axis=0), ax...  12 us
    ppermute x1, waiting for transfers between devices, from_behind(): return lax.ppermute(value, axis, pairs)  9.04 us
    ppermute x1, starting transfers between devices, from_behind(): return lax.ppermute(value, axis, pairs)  7.3 us
    all_to_all x1, starting transfers between devices, spread(): lax.all_to_all(partial_sums[2][None], 'sample', split_axis=1, concat_axis...  7.23 us
    all_to_all x1, waiting for transfers between devices, _place_lines(): lax.all_to_all(jnp.stack([message] * lax.axis_size('sample'), axis=0), ax...  7.12 us
    dot_general x3, matrix products, apply_weights(): jnp.einsum(form, weights, value_matrix, precision=lax.Precision.HIGHEST)  7 us
  transfers between devices with their start and end apart: 5, of which 4 were waited for; matrix products, arithmetic and copies ran while one was open for 24% of the time, Pallas kernels for 0%

profile of v1, /device:TPU:1, one launch (start us, length us, event | category | flops | bytes accessed | tf_op | source)
XLA Modules:
  0.0 130.0 jit_solution(4202689732081595624)
XLA Ops:
  0.0 2.3 %stack.2 = bf16[16,1,1,4,8192]{4,3,2,1,0:T(4,128)(2,1)} broadcast(bf16[4,8192]{1,0:T(4,128)(2,1)} %bitcast.177), dimensions={3,4} | broadcast | bytes 1114112 | tf_op jit(solution)/shard_map/stack | solution.py:14
  2.3 12.0 %all-to-all-start = ((bf16[16,1,1,4,8192]{4,3,2,1,0:T(4,128)(2,1)}), bf16[16,1,1,4,8192]{4,3,2,1,0:T(4,128)(2,1)S(1)}, u32[]{:S(2)}, u32[]{:S(2)}) async-start(bf16[16,1,1,4,8192]{4,3,2,1,0:T(4,128)(2,1)} %stack.2), calls=%async_computation | async-start | bytes 2097152 | tf_op jit(solution)/shard_map/all_to_all | solution.py:13
  14.3 1.2 copy.103
  15.5 7.3 %collective-permute-start = (bf16[1,128,2,1024]{1,3,2,0:T(8,128)(2,1)}, bf16[1,128,2,1024]{1,3,2,0:T(8,128)(2,1)S(1)}, u32[]{:S(2)}, u32[]{:S(2)}) collective-permute-start(bf16[1,128,2,1024]{1,3,2,0:T(8,128)(2,1)} %copy.103), channel_id=1, source_target_pairs={{0,496},{16,0},{32,16},{48,32},{64,48},{80,64},{96,80},{112,96},{1... | collective-permute-start | bytes 1572872 | tf_op jit(solution)/shard_map/ppermute | solution.py:26
  25.3 9.0 %collective-permute-done = bf16[1,128,2,1024]{1,3,2,0:T(8,128)(2,1)S(1)} collective-permute-done((bf16[1,128,2,1024]{1,3,2,0:T(8,128)(2,1)}, bf16[1,128,2,1024]{1,3,2,0:T(8,128)(2,1)S(1)}, u32[]{:S(2)}, u32[]{:S(2)}) %collective-permute-start) | collective-permute-done | bytes 524320 | tf_op jit(solution)/shard_map/ppermute | solution.py:26
  34.4 0.8 fusion.52
  35.1 7.1 %all-to-all-done = bf16[16,1,1,4,8192]{4,3,2,1,0:T(4,128)(2,1)S(1)} async-done(((bf16[16,1,1,4,8192]{4,3,2,1,0:T(4,128)(2,1)}), bf16[16,1,1,4,8192]{4,3,2,1,0:T(4,128)(2,1)S(1)}, u32[]{:S(2)}, u32[]{:S(2)}) %all-to-all-start) | async-done | bytes 1048608 | tf_op jit(solution)/shard_map/all_to_all | solution.py:13
  42.2 1.1 reshape.436
  43.3 1.0 bitcast_reduce_fusion
  44.4 1.0 bitcast_reduce_fusion.1
  45.4 3.3 %fusion.47 = (f32[16,4,8,8]{0,3,1,2:T(8,128)S(1)}, f32[16,4,8,8,128]{4,0,3,1,2:T(8,128)}, f32[16,4,8,8]{0,3,1,2:T(8,128)S(1)}, f32[16,4,8,8,128]{4,0,3,1,2:T(8,128)}) fusion(f32[16,4,8,8]{0,3,1,2:T(8,128)S(1)} %get-tuple-element.26, f32[8,128,16,4,8]{1,2,4,3,0:T(8,128)S(1)} %get-tuple-element.27, pred[128]{0:T(512)(128)(4,1)S(1)} %add_compare_fusion.1, ...), kind=kLoop, calls=%fused_computation.79 | loop fusion | flops 5234688 | bytes 8454400 | tf_op jit(solution)/shard_map/reduce_sum | solution.py:33
  48.8 0.7 reshape.440
  49.6 3.5 %all-to-all-start.2 = ((f32[16,1,256]{2,1,0:T(1,128)}), f32[16,1,256]{2,1,0:T(1,128)S(1)}, u32[]{:S(2)}, u32[]{:S(2)}) async-start(f32[16,1,256]{2,1,0:T(1,128)} %reshape.440), calls=%async_computation.2 | async-start | bytes 32768 | tf_op jit(solution)/shard_map/all_to_all | solution.py:110
  53.3 3.4 %fusion.11 = f32[16,4,8,8,128]{4,3,1,0,2:T(8,128)S(1)} fusion(bf16[128,8,128,1,1]{0,2,4,3,1:T(8,128)(2,1)S(1)} %bitcast.164, f32[16,4,8,8,128]{4,0,3,1,2:T(8,128)} %get-tuple-element.11), kind=kOutput, calls=%fused_computation.20 | convolution fusion | flops 805306368 | bytes 4456448 | tf_op jit(solution)/shard_map/urpyj,jpi->urpyi/dot_general | solution.py:34
  56.7 3.1 %fusion.14 = f32[16,4,8,8,128]{4,3,1,0,2:T(8,128)} fusion(bf16[128,8,128,1,1]{0,2,4,3,1:T(8,128)(2,1)S(1)} %bitcast.165, f32[16,4,8,8,128]{4,0,3,1,2:T(8,128)S(1)} %copy-done), kind=kOutput, calls=%fused_computation.21 | convolution fusion | flops 805306368 | bytes 4456448 | tf_op jit(solution)/shard_map/urpyj,jpi->urpyi/dot_general | solution.py:34
  59.9 0.7 reshape.442
  60.6 7.2 %all-to-all-start.3 = ((f32[16,1,256]{2,1,0:T(1,128)}), f32[16,1,256]{2,1,0:T(1,128)S(1)}, u32[]{:S(2)}, u32[]{:S(2)}) async-start(f32[16,1,256]{2,1,0:T(1,128)} %reshape.442), calls=%async_computation.3 | async-start | bytes 32768 | tf_op jit(solution)/shard_map/all_to_all | solution.py:111
  67.8 3.4 %fusion.2 = f32[1,16,4,64,128]{4,3,2,0,1:T(8,128)} fusion(f32[16,4,8,8,128]{4,3,1,0,2:T(8,128)} %fusion.14, f32[16,4,8,8,128]{4,3,1,0,2:T(8,128)S(1)} %fusion.11, f32[16,4,64]{2,1,0:T(4,128)S(1)} %copy.115, f32[16,4,64]{2,1,0:T(4,128)S(1)} %copy.110), kind=kLoop, calls=%fused_computation.4 | loop fusion | flops 1572864 | bytes 6324224 | tf_op jit(solution)/shard_map/add | solution.py:91
  71.3 3.9 %all-to-all-done.3 = f32[16,1,256]{2,1,0:T(1,128)S(1)} async-done(((f32[16,1,256]{2,1,0:T(1,128)}), f32[16,1,256]{2,1,0:T(1,128)S(1)}, u32[]{:S(2)}, u32[]{:S(2)}) %all-to-all-start.3) | async-done | bytes 16416 | tf_op jit(solution)/shard_map/all_to_all | solution.py:111
  75.2 3.9 %all-to-all-start.1 = ((f32[1,16,4,64,128]{4,3,2,0,1:T(8,128)}), f32[1,16,4,64,128]{4,3,2,0,1:T(8,128)S(1)}, u32[]{:S(2)}, u32[]{:S(2)}) async-start(f32[1,16,4,64,128]{4,3,2,0,1:T(8,128)} %fusion.2), calls=%async_computation.1 | async-start | bytes 4194304 | tf_op jit(solution)/shard_map/all_to_all | solution.py:109
  79.7 12.7 %fusion.19 = (bf16[260,1024]{1,0:T(8,128)(2,1)S(1)}, bf16[260,1024]{1,0:T(8,128)(2,1)S(1)}) fusion(bf16[1,4,2,1024]{3,2,1,0:T(2,128)(2,1)S(1)} %bitcast.179, bf16[1,256,2,1024]{3,2,1,0:T(2,128)(2,1)} %bitcast.163), kind=kLoop, calls=%fused_computation.28 | loop fusion | flops 2129920 | bytes 2129920 | tf_op jit(solution)/shard_map/slice | solution.py:64
  96.4 31.7 %all-to-all-done.1 = f32[1,16,4,64,128]{4,3,2,0,1:T(8,128)S(1)} async-done(((f32[1,16,4,64,128]{4,3,2,0,1:T(8,128)}), f32[1,16,4,64,128]{4,3,2,0,1:T(8,128)S(1)}, u32[]{:S(2)}, u32[]{:S(2)}) %all-to-all-start.1) | async-done | bytes 2097184 | tf_op jit(solution)/shard_map/all_to_all | solution.py:109
  128.1 0.7 fusion
  129.3 0.7 copy.129
  (59 shorter events, 7.3 us)
Async XLA Ops:
  0.0 14.3 %copy-start.1 = (bf16[1,128,2,1024]{3,2,1,0:T(2,128)(2,1)S(1)}, bf16[1,128,2,1024]{3,2,1,0:T(2,128)(2,1)}, u32[]{:S(2)}) copy-start(bf16[1,128,2,1024]{3,2,1,0:T(2,128)(2,1)} %param.12) | copy-start | bytes 1572868
  0.0 22.8 %copy-start.2 = (bf16[1,128,2,1024]{3,2,1,0:T(2,128)(2,1)S(1)}, bf16[1,128,2,1024]{3,2,1,0:T(2,128)(2,1)}, u32[]{:S(2)}) copy-start(bf16[1,128,2,1024]{3,2,1,0:T(2,128)(2,1)} %param.11) | copy-start | bytes 1572868
  2.3 21.0 %copy-start.6 = (s32[32]{0:T(128)S(1)}, s32[32]{0:T(128)}, u32[]{:S(2)}) copy-start(s32[32]{0:T(128)} %param.13) | copy-start | bytes 388
  2.3 39.9 %all-to-all-start = ((bf16[16,1,1,4,8192]{4,3,2,1,0:T(4,128)(2,1)}), bf16[16,1,1,4,8192]{4,3,2,1,0:T(4,128)(2,1)S(1)}, u32[]{:S(2)}, u32[]{:S(2)}) async-start(bf16[16,1,1,4,8192]{4,3,2,1,0:T(4,128)(2,1)} %stack.2), calls=%async_computation | async-start | bytes 2097152 | tf_op jit(solution)/shard_map/all_to_all | solution.py:13
  15.5 18.9 %collective-permute-start = (bf16[1,128,2,1024]{1,3,2,0:T(8,128)(2,1)}, bf16[1,128,2,1024]{1,3,2,0:T(8,128)(2,1)S(1)}, u32[]{:S(2)}, u32[]{:S(2)}) collective-permute-start(bf16[1,128,2,1024]{1,3,2,0:T(8,128)(2,1)} %copy.103), channel_id=1, source_target_pairs={{0,496},{16,0},{32,16},{48,32},{64,48},{80,64},{96,80},{112,96},{1... | collective-permute-start | bytes 1572872 | tf_op jit(solution)/shard_map/ppermute | solution.py:26
  35.1 8.2 %copy-start.3 = (bf16[128,1,1024]{0,2,1:T(8,128)(2,1)S(1)}, bf16[128,1,1024]{0,2,1:T(8,128)(2,1)}, u32[]{:S(2)}) copy-start(bf16[128,1,1024]{0,2,1:T(8,128)(2,1)} %get-tuple-element.17) | copy-start | bytes 786436
  49.6 11.0 %all-to-all-start.2 = ((f32[16,1,256]{2,1,0:T(1,128)}), f32[16,1,256]{2,1,0:T(1,128)S(1)}, u32[]{:S(2)}, u32[]{:S(2)}) async-start(f32[16,1,256]{2,1,0:T(1,128)} %reshape.440), calls=%async_computation.2 | async-start | bytes 32768 | tf_op jit(solution)/shard_map/all_to_all | solution.py:110
  53.3 3.4 %copy-start = (f32[16,4,8,8,128]{4,0,3,1,2:T(8,128)S(1)}, f32[16,4,8,8,128]{4,0,3,1,2:T(8,128)}, u32[]{:S(2)}) copy-start(f32[16,4,8,8,128]{4,0,3,1,2:T(8,128)} %get-tuple-element.29) | copy-start | bytes 6291460
  60.6 14.6 %all-to-all-start.3 = ((f32[16,1,256]{2,1,0:T(1,128)}), f32[16,1,256]{2,1,0:T(1,128)S(1)}, u32[]{:S(2)}, u32[]{:S(2)}) async-start(f32[16,1,256]{2,1,0:T(1,128)} %reshape.442), calls=%async_computation.3 | async-start | bytes 32768 | tf_op jit(solution)/shard_map/all_to_all | solution.py:111
  71.3 8.4 %copy-start.5 = (bf16[1,1,4,2,1024]{4,3,2,1,0:T(2,128)(2,1)S(1)}, bf16[1,1,4,2,1024]{4,3,2,1,0:T(2,128)(2,1)}, u32[]{:S(2)}) copy-start(bf16[1,1,4,2,1024]{4,3,2,1,0:T(2,128)(2,1)} %param.8) | copy-start | bytes 49156
  75.2 52.9 %all-to-all-start.1 = ((f32[1,16,4,64,128]{4,3,2,0,1:T(8,128)}), f32[1,16,4,64,128]{4,3,2,0,1:T(8,128)S(1)}, u32[]{:S(2)}, u32[]{:S(2)}) async-start(f32[1,16,4,64,128]{4,3,2,0,1:T(8,128)} %fusion.2), calls=%async_computation.1 | async-start | bytes 4194304 | tf_op jit(solution)/shard_map/all_to_all | solution.py:109
  79.7 12.9 %copy-start.4 = (bf16[1,1,4,8192]{3,2,1,0:T(4,128)(2,1)S(1)}, bf16[1,1,4,8192]{3,2,1,0:T(4,128)(2,1)}, u32[]{:S(2)}) copy-start(bf16[1,1,4,8192]{3,2,1,0:T(4,128)(2,1)} %param.7) | copy-start | bytes 196612
